TPU v7x, 512 devices: a whole 4x8x8 slice. The times are simulated.
512 devices in a mesh: req: 128 (over y, z, core), mlp: 4 (over x).
Axes of the slice: x: 4, y: 8, z: 8, core: 2. Of those that a mesh axis runs over, the one named last changes fastest.
Arguments:
- residual: bfloat16 [32768, 2048], P('req'), may hold values from -20 to 20
- query_rows: bfloat16 [32768, 2048], P('req', 'mlp'), may hold values from -6 to 6
- value_rows: bfloat16 [32768, 2048], P('req', 'mlp'), may hold values from -6 to 6
- forget_logit: float32 [32768, 2048], P('req', 'mlp'), may hold values from 0 to 40
- slot_kind: int32 [32768], P('req'), may hold values from 0 to 2, as said below
- head_gain: float32 [2048], P('mlp'), may hold values from 0.1 to 1.9
- out_weight: bfloat16 [2048, 2048], P('mlp', 'req'), may hold values from -0.125 to 0.125
- ffn_gain: float32 [2048], replicated, may hold values from 0.1 to 1.9
- gate_weight: bfloat16 [2048, 3072], P('req', 'mlp'), may hold values from -0.125 to 0.125
- up_weight: bfloat16 [2048, 3072], P('req', 'mlp'), may hold values from -0.125 to 0.125
- down_weight: bfloat16 [3072, 2048], P('mlp', 'req'), may hold values from -0.109375 to 0.109375
Outputs:
- layer_out: bfloat16 [32768, 2048], P('req', 'mlp')
Inputs may be any that keep to these rules, and one draw needn't show every extreme that they name: `slot_kind`: slots 0 to 24575 hold one prompt: slot 0 has kind 2, the others kind 1. Every other block of 256 slots holds short requests packed from its first slot, then empty slots; a short request has at most 32 tokens, the first request of each such block exactly 32. Over all 32768 slots exactly 26624 are live.
All inputs are finite; a program needn't handle non-finite values.
Results may differ from a plain program's by a relative error of at most 0.0163.
Values may be sent and summed in bfloat16 or wider, within the bound.
No kernel may reach another device: no remote copies, remote signals or barrier semaphores. Data moves between devices by JAX's collectives and lax.ppermute only.
A program may use at most 128 MiB of HBM per device.

v0:
```python
import jax
import jax.numpy as jnp
from jax import lax
from jax.sharding import PartitionSpec as P

HEAD = 128
SPAN = 32


def carried_in(part, axis, combine, identity):
    place = lax.axis_index(axis)
    gathered = jax.tree.map(lambda a: lax.all_gather(a, axis), part)
    state = jax.tree.map(lambda a, e: jnp.zeros_like(a) + jnp.asarray(e, a.dtype), part, identity)

    def one(hop, state):
        return combine(
            state, jax.tree.map(lambda a: lax.dynamic_index_in_dim(a, hop, 0, False), gathered)
        )

    return lax.fori_loop(0, place, one, state)


def span_step(passed_state, pieces):
    query_block, key_block, value_block, g_block = pieces
    top_precision = lax.Precision.HIGHEST
    inside_block_term = jnp.cumsum(g_block, axis=0)
    between_blocks_term = jnp.einsum(
        "owu,wuj->owj",
        query_block * jnp.exp(inside_block_term),
        passed_state,
        precision=top_precision,
    )
    length = g_block.shape[0]
    causal = jnp.arange(length)[:, None] >= jnp.arange(length)[None, :]
    causal = causal[:, :, None, None]
    gap_log = jnp.where(causal, inside_block_term[:, None] - inside_block_term[None, :], 0.0)
    decay_pairs = jnp.where(causal, jnp.exp(gap_log), 0.0)
    scores = jnp.einsum(
        "tnk,tsnk->tsn", query_block, decay_pairs * key_block[None], precision=top_precision
    )
    intra_part = jnp.einsum("tsn,snv->tnv", scores, value_block, precision=top_precision)
    final_decay_sum = inside_block_term[-1]
    updated_state = jnp.exp(final_decay_sum)[:, :, None] * passed_state + jnp.einsum(
        "weq,wel->eql",
        key_block * jnp.exp(final_decay_sum[None] - inside_block_term),
        value_block,
        precision=top_precision,
    )
    return (updated_state, between_blocks_term + intra_part)


def compose(earlier, later):
    return (
        earlier[0] * later[0],
        later[0][:, :, None] * earlier[1] + later[1],
        earlier[2] + later[2],
    )


def on_device(
    residual,
    query_rows,
    value_rows,
    forget_logit,
    slot_kind,
    head_gain,
    out_weight,
    ffn_gain,
    gate_weight,
    up_weight,
    down_weight,
):
    slot_total = residual.shape[0]
    quarter = query_rows.shape[1]
    heads_here = quarter // HEAD
    live_mask = slot_kind > 0
    first_mask = slot_kind == 2
    log_forget = jnp.where(
        first_mask[:, None],
        -80.0,
        jnp.where(live_mask[:, None], -jax.nn.softplus(-forget_logit), 0.0),
    )
    key_gate = jnp.where(live_mask[:, None], jax.nn.sigmoid(-forget_logit), 0.0)
    shape4 = (slot_total // SPAN, SPAN, heads_here, HEAD)
    q_all = query_rows.astype(jnp.float32).reshape(shape4)
    v_all = value_rows.astype(jnp.float32).reshape(shape4)
    k_all = key_gate.reshape(shape4)
    g_all = log_forget.reshape(shape4)
    zero_state = jnp.zeros((heads_here, HEAD, HEAD), jnp.float32)
    decay_whole = jnp.exp(jnp.sum(log_forget, axis=0)).reshape(heads_here, HEAD)
    live_count = jnp.sum(live_mask.astype(jnp.float32))
    neutral = (jnp.ones_like(decay_whole), jnp.zeros_like(zero_state), jnp.zeros((), jnp.float32))
    end_state, local_out = lax.scan(span_step, zero_state, (q_all, k_all, v_all, g_all))
    leading_decay = carried_in((decay_whole, end_state, live_count), "req", compose, neutral)
    within_all = jnp.cumsum(g_all, axis=1)
    block_total = within_all[:, -1]
    before_block = jnp.cumsum(block_total, axis=0) - block_total
    query_damped = q_all * jnp.exp(within_all + before_block[:, None])
    heads_out = local_out + jnp.einsum(
        "mosf,sfl->mosl", query_damped, leading_decay[1], precision=lax.Precision.HIGHEST
    )
    heads_out = heads_out.reshape(slot_total, heads_here, HEAD)
    mean_sq = jnp.mean(heads_out * heads_out, axis=-1, keepdims=True)
    head_normed = (
        heads_out / jnp.sqrt(mean_sq + 1e-06) * head_gain.reshape(heads_here, HEAD)
    ).astype(jnp.bfloat16)
    head_normed = head_normed.reshape(slot_total, quarter)
    partial_rows = jnp.dot(
        head_normed,
        lax.all_gather(out_weight, "req", axis=1, tiled=True),
        preferred_element_type=jnp.float32,
    )
    mixed_sum = lax.psum(partial_rows.astype(jnp.bfloat16), "mlp").astype(jnp.float32)
    stream = (residual.astype(jnp.float32) + mixed_sum).astype(jnp.bfloat16)
    my_cols = lax.axis_index("mlp") * quarter
    rows_f = stream.astype(jnp.float32)
    ffn_in = (
        rows_f / jnp.sqrt(jnp.mean(rows_f * rows_f, axis=-1, keepdims=True) + 1e-05) * ffn_gain
    ).astype(jnp.bfloat16)
    gate_acc = jnp.dot(
        ffn_in,
        lax.all_gather(gate_weight, "req", axis=0, tiled=True),
        preferred_element_type=jnp.float32,
    )
    up_acc = jnp.dot(
        ffn_in,
        lax.all_gather(up_weight, "req", axis=0, tiled=True),
        preferred_element_type=jnp.float32,
    )
    hidden = (jax.nn.silu(gate_acc) * up_acc).astype(jnp.bfloat16)
    terms = jnp.dot(
        hidden,
        lax.all_gather(down_weight, "req", axis=1, tiled=True),
        preferred_element_type=jnp.float32,
    )
    ffn_out = lax.psum_scatter(
        terms.astype(jnp.bfloat16), "mlp", scatter_dimension=1, tiled=True
    ).astype(jnp.float32)
    own_cols = lax.dynamic_slice_in_dim(stream, my_cols, quarter, 1).astype(jnp.float32)
    result = (own_cols + ffn_out).astype(jnp.bfloat16)
    layer_out = jnp.where(live_mask[:, None], result, jnp.zeros_like(result))
    return layer_out


def solution(mesh):
    return jax.shard_map(
        on_device,
        mesh=mesh,
        in_specs=(
            P("req", None),
            P("req", "mlp"),
            P("req", "mlp"),
            P("req", "mlp"),
            P("req"),
            P("mlp"),
            P("mlp", "req"),
            P(),
            P("req", "mlp"),
            P("req", "mlp"),
            P("mlp", "req"),
        ),
        out_specs=P("req", "mlp"),
        check_vma=False,
    )
```

profile of v0, /device:TPU:8, one launch (start us, length us, event | category | flops | bytes accessed | tf_op | source)
XLA Modules:
  0.0 706.2 jit_solution(7420464183667757412)
XLA Ops:
  6.5 0.7 broadcast_compare_fusion
  7.3 1.6 fusion.38
  9.6 50.4 %while.27 = (s32[]{:T(128)}, f32[4,128,128]{2,1,0:T(8,128)S(1)}, f32[8,32,4,128]{3,1,0,2:T(8,128)S(1)}, f32[8,32,4,128]{3,2,1,0:T(4,128)S(1)}, f32[8,32,4,128]{3...) while((s32[]{:T(128)}, f32[4,128,128]{2,1,0:T(8,128)S(1)}, ...), condition=%wide.region_2.3_spmd.clone, body=%wide.region_0.2_spmd.clone.sunk | while | flops 65848320 | bytes 6453368 | solution.py:93
  9.7 1.6 select_multiply_fusion.2
  11.3 3.3 fusion.68
  15.2 0.6 convolution_add_fusion.2
  16.0 1.6 select_multiply_fusion.2
  17.6 3.3 fusion.68
  21.5 0.6 convolution_add_fusion.2
  22.3 1.6 select_multiply_fusion.2
  23.9 3.3 fusion.68
  27.8 0.6 convolution_add_fusion.2
  28.6 1.6 select_multiply_fusion.2
  30.2 3.3 fusion.68
  34.1 0.6 convolution_add_fusion.2
  34.9 1.6 select_multiply_fusion.2
  36.5 3.3 fusion.68
  40.4 0.6 convolution_add_fusion.2
  41.2 1.6 select_multiply_fusion.2
  42.8 3.3 fusion.68
  46.7 0.6 convolution_add_fusion.2
  47.5 1.6 select_multiply_fusion.2
  49.1 3.3 fusion.68
  53.0 0.6 convolution_add_fusion.2
  53.8 1.6 select_multiply_fusion.2
  55.4 3.3 fusion.68
  59.3 0.6 convolution_add_fusion.2
  60.0 0.7 copy-done
  60.7 0.7 all-gather.7.cloned.1.call-update
  61.5 0.4 fusion.27
  62.4 56.7 %all_gather.23 = f32[128,4,128]{2,1,0:T(4,128)S(1)} all-gather(f32[1,4,128]{2,1,0:T(4,128)S(1)} %exponential_bitcast_fusion), channel_id=1, replica_groups=mesh['req'=128,'mlp'=4] {'req'}, dimensions={0}, use_global_device_ids=true | all-gather | bytes 264192 | tf_op jit(solution)/shard_map/all_gather | solution.py:12
  119.1 87.6 %all-gather.15.cloned.1.call-done = f32[512,128,128]{2,1,0:T(8,128)} async-done(((f32[4,128,128]{2,1,0:T(8,128)}), f32[512,128,128]{2,1,0:T(8,128)}) %all-gather.15.cloned.1.call-update) | async-done | bytes 33554448 | tf_op jit(solution)/shard_map/all_gather | solution.py:12
  206.7 18.6 %while.26 = (s32[]{:T(128)}, f32[4,128,128]{2,1,0:T(8,128)S(1)}, s32[]{:T(128)}, f32[128,4,128]{2,1,0:T(4,128)S(1)}, f32[128,4,128,128]{3,2,1,0:T(8,128)}, /*index=5*/s32[]{:T(128)}, s32[]{:T(128)}, s32[]{:T(128)}) while((s32[]{:T(128)}, f32[4,128,128]{2,1,0:T(8,128)S(1)}, s32[]{:T(128)}, f32[128,4,128]{2,1,0:T(4,128)S(1)}, ...), condition=%wide.region_5.6_spmd, body=%wide.region_4.5_spmd.sunk | while | flops 131077 | bytes 792703 | solution.py:20
  206.7 1.1 bitcast_add_fusion.2
  207.9 1.1 bitcast_add_fusion.2
  209.0 1.1 bitcast_add_fusion.2
  210.2 1.1 bitcast_add_fusion.2
  211.4 1.1 bitcast_add_fusion.2
  212.5 1.1 bitcast_add_fusion.2
  213.7 1.1 bitcast_add_fusion.2
  214.9 1.1 bitcast_add_fusion.2
  216.0 1.1 bitcast_add_fusion.2
  217.2 1.1 bitcast_add_fusion.2
  218.3 1.1 bitcast_add_fusion.2
  219.5 1.1 bitcast_add_fusion.2
  220.7 1.1 bitcast_add_fusion.2
  221.8 1.1 bitcast_add_fusion.2
  223.0 1.1 bitcast_add_fusion.2
  224.2 1.1 bitcast_add_fusion.2
  225.3 0.6 fusion.40
  226.6 63.5 %all-gather.7.cloned.1.call-done = bf16[512,2048]{0,1:T(8,128)(2,1)} async-done(((bf16[512,16]{0,1:T(8,128)(2,1)}), bf16[512,2048]{0,1:T(8,128)(2,1)}) %all-gather.7.cloned.1.call-update) | async-done | bytes 2097168 | tf_op jit(solution)/shard_map/all_gather | solution.py:110
  290.5 3.4 convolution_convert_fusion
  294.0 0.5 all-gather.9.cloned.1.call-update
  294.6 0.5 all-gather.11.cloned.1.call-update
  295.2 0.5 all-gather.13.cloned.1.call-update
  295.9 114.3 %all-reduce.2.cloned.1.call-done = bf16[256,2048]{1,0:T(8,128)(2,1)} async-done(((bf16[256,2048]{1,0:T(8,128)(2,1)}), bf16[256,2048]{1,0:T(8,128)(2,1)}) %all-reduce.2.cloned.1.call-update) | async-done | bytes 1048592 | tf_op jit(solution)/shard_map/psum | solution.py:113
  410.2 1.7 fusion.18
  412.0 85.4 %all-gather.9.cloned.1.call-done = bf16[2048,768]{1,0:T(8,128)(2,1)} async-done(((bf16[16,768]{1,0:T(8,128)(2,1)}), bf16[2048,768]{1,0:T(8,128)(2,1)}) %all-gather.9.cloned.1.call-update) | async-done | bytes 3145744 | tf_op jit(solution)/shard_map/all_gather | solution.py:122
  497.4 2.9 fusion.36
  500.3 80.7 %all-gather.11.cloned.1.call-done = bf16[2048,768]{1,0:T(8,128)(2,1)} async-done(((bf16[16,768]{1,0:T(8,128)(2,1)}), bf16[2048,768]{1,0:T(8,128)(2,1)}) %all-gather.11.cloned.1.call-update) | async-done | bytes 3145744 | tf_op jit(solution)/shard_map/all_gather | solution.py:127
  581.1 83.7 %all-gather.13.cloned.1.call-done = bf16[768,2048]{0,1:T(8,128)(2,1)} async-done(((bf16[768,16]{0,1:T(8,128)(2,1)}), bf16[768,2048]{0,1:T(8,128)(2,1)}) %all-gather.13.cloned.1.call-update) | async-done | bytes 3145744 | tf_op jit(solution)/shard_map/all_gather | solution.py:133
  664.8 6.1 convolution_convert_fusion.1
  670.9 26.7 %reduce-scatter.2.cloned.1.call-done = bf16[256,512]{1,0:T(8,128)(2,1)} async-done(((bf16[256,2048]{1,0:T(8,128)(2,1)}), bf16[256,512]{1,0:T(8,128)(2,1)}) %reduce-scatter.2.cloned.1.call-update) | async-done | bytes 262160 | tf_op jit(solution)/shard_map/reduce_scatter | solution.py:136
  697.6 1.8 fusion.30
  (120 shorter events, 8.3 us)
Async XLA Ops:
  6.5 2.5 copy-start.2
  6.5 200.1 %all-gather.15.cloned.1.call-start = ((), (), s32[]{:S(2)}) async-start(), calls=%async_computation.7 | async-start | bytes 33816576 | tf_op jit(solution)/shard_map/all_gather | solution.py:12
  7.3 2.1 copy-start.3
  60.0 0.7 copy-start
  60.7 229.5 %all-gather.7.cloned.1.call-start = ((), (), s32[]{:S(2)}) async-start(), calls=%async_computation.1 | async-start | bytes 2113536 | tf_op jit(solution)/shard_map/all_gather | solution.py:110
  61.4 348.8 %all-reduce.2.cloned.1.call-start = ((), (), s32[]{:S(2)}) async-start(), calls=%async_computation.2 | async-start | bytes 2097152 | tf_op jit(solution)/shard_map/psum | solution.py:113
  225.3 65.2 %copy-start.5 = (f32[512]{0:T(512)S(1)}, f32[512]{0:T(512)}, u32[]{:S(2)}) copy-start(f32[512]{0:T(512)} %param.20) | copy-start | bytes 6148
  290.5 119.7 %copy-start.1 = (bf16[256,2048]{1,0:T(8,128)(2,1)S(1)}, bf16[256,2048]{1,0:T(8,128)(2,1)}, u32[]{:S(2)}) copy-start(bf16[256,2048]{1,0:T(8,128)(2,1)} %param.15) | copy-start | bytes 3145732
  293.9 203.5 %copy-start.4 = (f32[2048]{0:T(1024)S(1)}, f32[2048]{0:T(1024)}, u32[]{:S(2)}) copy-start(f32[2048]{0:T(1024)} %param.22) | copy-start | bytes 24580
  293.9 203.4 %all-gather.9.cloned.1.call-start = ((), (), s32[]{:S(2)}) async-start(), calls=%async_computation.3 | async-start | bytes 3170304 | tf_op jit(solution)/shard_map/all_gather | solution.py:122
  294.5 286.5 %all-gather.11.cloned.1.call-start = ((), (), s32[]{:S(2)}) async-start(), calls=%async_computation.4 | async-start | bytes 3170304 | tf_op jit(solution)/shard_map/all_gather | solution.py:127
  295.1 369.7 %all-gather.13.cloned.1.call-start = ((), (), s32[]{:S(2)}) async-start(), calls=%async_computation.5 | async-start | bytes 3170304 | tf_op jit(solution)/shard_map/all_gather | solution.py:133
  295.7 401.9 %reduce-scatter.2.cloned.1.call-start = ((), (), s32[]{:S(2)}) async-start(), calls=%async_computation.6 | async-start | bytes 1310720 | tf_op jit(solution)/shard_map/reduce_scatter | solution.py:136
Sparse Core Ops, SparseCore 0:
  60.8 145.7 all-gather.14
  209.8 80.3 all-gather.6
  294.1 116.1 all-reduce.1
  413.2 84.1 all-gather.8
  500.3 80.6 all-gather.10
  584.0 80.6 all-gather.12
  671.0 26.5 reduce-scatter.1
where the time goes:
time: 710 us; the launch traced here: 706 us
  waiting for transfers between devices  544 us (77%)
  blocking collectives  56.7 us (8%)
  matrix products  49.3 us (7%)
  other arithmetic  38 us (5%)
  between operations  13.7 us (2%)
    psum x1, waiting for transfers between devices, on_device(): lax.psum(partial_rows.astype(jnp.bfloat16), 'mlp').astype(jnp.float32)  114 us
    all_gather x1, waiting for transfers between devices, carried_in(): gathered = jax.tree.map(lambda a: lax.all_gather(a, axis), part)  87.6 us
    all_gather x1, waiting for transfers between devices, on_device(): lax.all_gather(gate_weight, 'req', axis=0, tiled=True)  85.4 us
    all_gather x1, waiting for transfers between devices, on_device(): lax.all_gather(down_weight, 'req', axis=1, tiled=True)  83.7 us
    all_gather x1, waiting for transfers between devices, on_device(): lax.all_gather(up_weight, 'req', axis=0, tiled=True)  80.7 us
    all_gather x1, waiting for transfers between devices, on_device(): lax.all_gather(out_weight, 'req', axis=1, tiled=True)  63.5 us
    all_gather x1, blocking collectives, carried_in(): gathered = jax.tree.map(lambda a: lax.all_gather(a, axis), part)  56.7 us
    dot_general x8, matrix products, span_step(): jnp.einsum('tnk,tsnk->tsn', query_block, decay_pairs * key_block[None], p...  26.8 us
  transfers between devices with their start and end apart: 7, of which 7 were waited for; matrix products, arithmetic and copies ran while one was open for 4% of the time, Pallas kernels for 0%

commit v1 on v0

--- a/solution.py
+++ b/solution.py
@@ -130,7 +130,9 @@
     hidden = (jax.nn.silu(gate_acc) * up_acc).astype(jnp.bfloat16)
     terms = jnp.dot(
         hidden,
-        lax.all_gather(down_weight, "req", axis=1, tiled=True),
+        jnp.concatenate(
+            lax.all_to_all(jnp.stack([down_weight] * lax.axis_size("req")), "req", 0, 0), axis=1
+        ),
         preferred_element_type=jnp.float32,
     )
     ffn_out = lax.psum_scatter(

time: 710 us -> 632 us (0.89)
  waiting for transfers between devices: 544 us -> 390 us
  starting transfers between devices: 0.42 us -> 72.4 us
    all_gather x1 -> x0, waiting for transfers between devices: 83.7 us -> none  [on_device(): lax.all_gather(down_weight, 'req', axis=1, tiled=True)]
    psum x1, waiting for transfers between devices: 114 us -> 40.7 us  [on_device(): lax.psum(partial_rows.astype(jnp.bfloat16), 'mlp').astype(jnp.float32)]
    all_to_all x0 -> x1, starting transfers between devices: none -> 72 us  [on_device(): lax.all_to_all(jnp.stack([down_weight] * lax.axis_size('req')), 'req', 0, 0)]
  transfers between devices with their start and end apart: 7 -> 7, of which waited for: 7 -> 6; matrix products, arithmetic and copies ran while one was open for 4% -> 5% of each run, Pallas kernels for 0% -> 0%
where the time goes in v1:
time: 632 us; the launch traced here: 628 us
  waiting for transfers between devices  390 us (62%)
  starting transfers between devices  72.4 us (11%)
  blocking collectives  56.7 us (9%)
  matrix products  49.9 us (8%)
  other arithmetic  39.2 us (6%)
  between operations  13.7 us (2%)
    all_gather x1, waiting for transfers between devices, on_device(): lax.all_gather(gate_weight, 'req', axis=0, tiled=True)  90.1 us
    all_gather x1, waiting for transfers between devices, carried_in(): gathered = jax.tree.map(lambda a: lax.all_gather(a, axis), part)  87.6 us
    all_gather x1, waiting for transfers between devices, on_device(): lax.all_gather(up_weight, 'req', axis=0, tiled=True)  79.6 us
    all_to_all x1, starting transfers between devices, on_device(): lax.all_to_all(jnp.stack([down_weight] * lax.axis_size('req')), 'req', 0, 0)  72 us
    all_gather x1, waiting for transfers between devices, on_device(): lax.all_gather(out_weight, 'req', axis=1, tiled=True)  63.6 us
    all_gather x1, blocking collectives, carried_in(): gathered = jax.tree.map(lambda a: lax.all_gather(a, axis), part)  56.7 us
    psum x1, waiting for transfers between devices, on_device(): lax.psum(partial_rows.astype(jnp.bfloat16), 'mlp').astype(jnp.float32)  40.7 us
    reduce_scatter x1, waiting for transfers between devices, on_device(): lax.psum_scatter(terms.astype(jnp.bfloat16), 'mlp', scatter_dimension=1,...  26.8 us
  transfers between devices with their start and end apart: 7, of which 6 were waited for; matrix products, arithmetic and copies ran while one was open for 5% of the time, Pallas kernels for 0%

profile of v1, /device:TPU:8, one launch (start us, length us, event | category | flops | bytes accessed | tf_op | source)
XLA Modules:
  0.0 627.6 jit_solution(7775289187042406453)
XLA Ops:
  6.5 0.7 broadcast_compare_fusion
  7.3 1.6 fusion.38
  9.6 50.4 %while.27 = (s32[]{:T(128)}, f32[4,128,128]{2,1,0:T(8,128)S(1)}, f32[8,32,4,128]{3,1,0,2:T(8,128)S(1)}, f32[8,32,4,128]{3,2,1,0:T(4,128)S(1)}, f32[8,32,4,128]{3...) while((s32[]{:T(128)}, f32[4,128,128]{2,1,0:T(8,128)S(1)}, ...), condition=%wide.region_2.3_spmd.clone, body=%wide.region_0.2_spmd.clone.sunk | while | flops 65848320 | bytes 6453368 | solution.py:93
  9.7 1.6 select_multiply_fusion.2
  11.3 3.3 fusion.68
  15.2 0.6 convolution_add_fusion.2
  16.0 1.6 select_multiply_fusion.2
  17.6 3.3 fusion.68
  21.5 0.6 convolution_add_fusion.2
  22.3 1.6 select_multiply_fusion.2
  23.9 3.3 fusion.68
  27.8 0.6 convolution_add_fusion.2
  28.6 1.6 select_multiply_fusion.2
  30.2 3.3 fusion.68
  34.1 0.6 convolution_add_fusion.2
  34.9 1.6 select_multiply_fusion.2
  36.5 3.3 fusion.68
  40.4 0.6 convolution_add_fusion.2
  41.2 1.6 select_multiply_fusion.2
  42.8 3.3 fusion.68
  46.7 0.6 convolution_add_fusion.2
  47.5 1.6 select_multiply_fusion.2
  49.1 3.3 fusion.68
  53.0 0.6 convolution_add_fusion.2
  53.8 1.6 select_multiply_fusion.2
  55.4 3.3 fusion.68
  59.3 0.6 convolution_add_fusion.2
  60.0 0.7 copy-done
  60.7 0.7 all-gather.6.cloned.1.call-update
  61.5 0.4 fusion.27
  62.4 56.7 %all_gather.20 = f32[128,4,128]{2,1,0:T(4,128)S(1)} all-gather(f32[1,4,128]{2,1,0:T(4,128)S(1)} %exponential_bitcast_fusion), channel_id=1, replica_groups=mesh['req'=128,'mlp'=4] {'req'}, dimensions={0}, use_global_device_ids=true | all-gather | bytes 264192 | tf_op jit(solution)/shard_map/all_gather | solution.py:12
  119.1 87.6 %all-gather.12.cloned.1.call-done = f32[512,128,128]{2,1,0:T(8,128)} async-done(((f32[4,128,128]{2,1,0:T(8,128)}), f32[512,128,128]{2,1,0:T(8,128)}) %all-gather.12.cloned.1.call-update) | async-done | bytes 33554448 | tf_op jit(solution)/shard_map/all_gather | solution.py:12
  206.7 18.6 %while.26 = (s32[]{:T(128)}, f32[4,128,128]{2,1,0:T(8,128)S(1)}, s32[]{:T(128)}, f32[128,4,128]{2,1,0:T(4,128)S(1)}, f32[128,4,128,128]{3,2,1,0:T(8,128)}, /*index=5*/s32[]{:T(128)}, s32[]{:T(128)}, s32[]{:T(128)}) while((s32[]{:T(128)}, f32[4,128,128]{2,1,0:T(8,128)S(1)}, s32[]{:T(128)}, f32[128,4,128]{2,1,0:T(4,128)S(1)}, ...), condition=%wide.region_5.6_spmd, body=%wide.region_4.5_spmd.sunk | while | flops 131077 | bytes 792703 | solution.py:20
  206.7 1.1 bitcast_add_fusion.2
  207.9 1.1 bitcast_add_fusion.2
  209.0 1.1 bitcast_add_fusion.2
  210.2 1.1 bitcast_add_fusion.2
  211.4 1.1 bitcast_add_fusion.2
  212.5 1.1 bitcast_add_fusion.2
  213.7 1.1 bitcast_add_fusion.2
  214.8 1.1 bitcast_add_fusion.2
  216.0 1.1 bitcast_add_fusion.2
  217.2 1.1 bitcast_add_fusion.2
  218.3 1.1 bitcast_add_fusion.2
  219.5 1.1 bitcast_add_fusion.2
  220.6 1.1 bitcast_add_fusion.2
  221.8 1.1 bitcast_add_fusion.2
  223.0 1.1 bitcast_add_fusion.2
  224.1 1.1 bitcast_add_fusion.2
  225.3 0.6 fusion.40
  226.6 63.6 %all-gather.6.cloned.1.call-done = bf16[512,2048]{0,1:T(8,128)(2,1)} async-done(((bf16[512,16]{0,1:T(8,128)(2,1)}), bf16[512,2048]{0,1:T(8,128)(2,1)}) %all-gather.6.cloned.1.call-update) | async-done | bytes 2097168 | tf_op jit(solution)/shard_map/all_gather | solution.py:110
  290.5 3.3 convolution_convert_fusion
  293.9 0.5 all-gather.8.cloned.1.call-update
  294.5 1.9 stack.2
  296.4 72.0 %all-to-all-start = ((bf16[128,768,16]{1,2,0:T(8,128)(2,1)}), bf16[128,768,16]{1,2,0:T(8,128)(2,1)S(1)}, u32[]{:S(2)}, u32[]{:S(2)}) async-start(bf16[128,768,16]{1,2,0:T(8,128)(2,1)} %stack.2), calls=%async_computation | async-start | bytes 6291456 | tf_op jit(solution)/shard_map/all_to_all | solution.py:134
  368.4 0.5 all-gather.10.cloned.1.call-update
  369.2 40.7 %all-reduce.2.cloned.1.call-done = bf16[256,2048]{1,0:T(8,128)(2,1)} async-done(((bf16[256,2048]{1,0:T(8,128)(2,1)}), bf16[256,2048]{1,0:T(8,128)(2,1)}) %all-reduce.2.cloned.1.call-update) | async-done | bytes 1048592 | tf_op jit(solution)/shard_map/psum | solution.py:113
  409.9 2.9 fusion.18
  412.8 90.1 %all-gather.8.cloned.1.call-done = bf16[2048,768]{1,0:T(8,128)(2,1)} async-done(((bf16[16,768]{1,0:T(8,128)(2,1)}), bf16[2048,768]{1,0:T(8,128)(2,1)}) %all-gather.8.cloned.1.call-update) | async-done | bytes 3145744 | tf_op jit(solution)/shard_map/all_gather | solution.py:122
  502.9 4.1 fusion.36
  507.0 79.6 %all-gather.10.cloned.1.call-done = bf16[2048,768]{1,0:T(8,128)(2,1)} async-done(((bf16[16,768]{1,0:T(8,128)(2,1)}), bf16[2048,768]{1,0:T(8,128)(2,1)}) %all-gather.10.cloned.1.call-update) | async-done | bytes 3145744 | tf_op jit(solution)/shard_map/all_gather | solution.py:127
  586.6 5.6 convolution_convert_fusion.1
  592.2 26.8 %reduce-scatter.2.cloned.1.call-done = bf16[256,512]{1,0:T(8,128)(2,1)} async-done(((bf16[256,2048]{1,0:T(8,128)(2,1)}), bf16[256,512]{1,0:T(8,128)(2,1)}) %reduce-scatter.2.cloned.1.call-update) | async-done | bytes 262160 | tf_op jit(solution)/shard_map/reduce_scatter | solution.py:138
  618.9 1.8 fusion.30
  (120 shorter events, 8.2 us)
Async XLA Ops:
  6.5 2.5 copy-start.1
  6.5 200.1 %all-gather.12.cloned.1.call-start = ((), (), s32[]{:S(2)}) async-start(), calls=%async_computation.7 | async-start | bytes 33816576 | tf_op jit(solution)/shard_map/all_gather | solution.py:12
  7.3 2.1 copy-start.2
  60.0 0.7 copy-start
  60.7 229.5 %all-gather.6.cloned.1.call-start = ((), (), s32[]{:S(2)}) async-start(), calls=%async_computation.2 | async-start | bytes 2113536 | tf_op jit(solution)/shard_map/all_gather | solution.py:110
  61.4 348.5 %all-reduce.2.cloned.1.call-start = ((), (), s32[]{:S(2)}) async-start(), calls=%async_computation.3 | async-start | bytes 2097152 | tf_op jit(solution)/shard_map/psum | solution.py:113
  225.3 65.2 %copy-start.5 = (f32[512]{0:T(512)S(1)}, f32[512]{0:T(512)}, u32[]{:S(2)}) copy-start(f32[512]{0:T(512)} %param.20) | copy-start | bytes 6148
  290.5 3.9 copy-start.3
  293.9 209.0 %all-gather.8.cloned.1.call-start = ((), (), s32[]{:S(2)}) async-start(), calls=%async_computation.4 | async-start | bytes 3170304 | tf_op jit(solution)/shard_map/all_gather | solution.py:122
  296.4 210.6 %all-to-all-start = ((bf16[128,768,16]{1,2,0:T(8,128)(2,1)}), bf16[128,768,16]{1,2,0:T(8,128)(2,1)S(1)}, u32[]{:S(2)}, u32[]{:S(2)}) async-start(bf16[128,768,16]{1,2,0:T(8,128)(2,1)} %stack.2), calls=%async_computation | async-start | bytes 6291456 | tf_op jit(solution)/shard_map/all_to_all | solution.py:134
  368.3 134.5 %copy-start.4 = (f32[2048]{0:T(1024)S(1)}, f32[2048]{0:T(1024)}, u32[]{:S(2)}) copy-start(f32[2048]{0:T(1024)} %param.22) | copy-start | bytes 24580
  368.4 218.2 %all-gather.10.cloned.1.call-start = ((), (), s32[]{:S(2)}) async-start(), calls=%async_computation.5 | async-start | bytes 3170304 | tf_op jit(solution)/shard_map/all_gather | solution.py:127
  368.9 250.0 %reduce-scatter.2.cloned.1.call-start = ((), (), s32[]{:S(2)}) async-start(), calls=%async_computation.6 | async-start | bytes 1310720 | tf_op jit(solution)/shard_map/reduce_scatter | solution.py:138
Sparse Core Ops, SparseCore 0:
  60.8 145.7 all-gather.11
  209.8 80.3 all-gather.5
  294.0 115.8 all-reduce.1
  412.9 89.9 all-gather.7
  505.8 80.6 all-gather.9
  592.3 26.6 reduce-scatter.1
